TPU v7x, 256 devices: a whole 4x4x8 slice. The times are simulated.
256 devices in a mesh: space: 32 (over z_hi, x, core), scen: 8 (over y, z_lo).
Axes of the slice: x: 4, y: 4, z: 8 (z_hi: 4, z_lo: 2; z = z_hi * 2 + z_lo), core: 2. Of those that a mesh axis runs over, the one named last changes fastest.
Arguments:
- concentration: float32 [8, 8, 6, 384, 384], P('scen', None, None, 'space'), may hold values from -6 to 6
- emissions: float32 [8, 6, 384, 384], P('scen', None, 'space'), may hold values from -3 to 3
- courant: float32 [2, 8, 6, 384, 384], P(None, None, None, 'space'), may hold values from -0.9 to 0.9
- tile_source: int32 [8640], P('space'), may hold values from 0 to 215, as said below
- tile_target: int32 [8640], P('space'), may hold values from 0 to 1023, as said below
- intersection: bfloat16 [8640, 128, 128], P('space'), may hold values from 0 to 0.0625
Outputs:
- transported: float32 [8, 8, 6, 384, 384], P('scen', None, None, 'space')
- regridded: float32 [8, 8, 1024, 128], P('scen', None, 'space')
- ensemble_moments: float32 [2, 8, 1024, 128], P(None, None, 'space')
Inputs may be any that keep to these rules, and one draw needn't show every extreme that they name: `tile_source`: every source block of a row band is named by at least one of the band's tiles. `tile_target`: latitude band b holds target blocks b * 32 to (b+1) * 32 - 1. The 270 tiles of one row band name at most 16 blocks of any one latitude band and at least 8 of every latitude band but one, which receives exactly 16 tiles from every row band. Every target block is named by some tile.
All inputs are finite; a program needn't handle non-finite values.
Results may differ from a plain program's by a relative error of at most 0.0027.
Values sent between devices are 32-bit elements; how exact they have to be, the bound alone decides.
No kernel may reach another device: no remote copies, remote signals or barrier semaphores. Data moves between devices by JAX's collectives and lax.ppermute only.
A program may use at most 128 MiB of HBM per device.

v0:
```python
import jax
import jax.numpy as jnp
from jax import lax
from jax.sharding import PartitionSpec as P

TGT_DEV = 32


def broadcast(value, axis, source):
    kept = jnp.where(lax.axis_index(axis) == source, value, 0).astype(value.dtype)
    return lax.psum(kept, axis)


def from_behind(block, axis, distance):
    devices = range(lax.axis_size(axis))
    route = [((i - distance) % len(devices), i) for i in devices]
    return lax.ppermute(block, axis, route)


def parabola_sweep(padded, courant_faces, sweep_axis):
    cells_along = padded.shape[sweep_axis] - 6

    def window(values_in, first_cell, length):
        return lax.slice_in_dim(values_in, first_cell, first_cell + length, axis=sweep_axis)

    edge_values = 7.0 / 12.0 * (
        window(padded, 1, cells_along + 3) + window(padded, 2, cells_along + 3)
    ) - 1.0 / 12.0 * (window(padded, 0, cells_along + 3) + window(padded, 3, cells_along + 3))
    left_edge = window(edge_values, 0, cells_along + 2)
    right_edge = window(edge_values, 1, cells_along + 2)
    centre = window(padded, 2, cells_along + 2)
    slopes = right_edge - left_edge
    curvature = 6.0 * centre - 3.0 * (left_edge + right_edge)
    backward = -courant_faces
    upwind_left = courant_faces * (
        window(right_edge, 0, cells_along + 1)
        - 0.5
        * courant_faces
        * (
            window(slopes, 0, cells_along + 1)
            - (1.0 - 2.0 * courant_faces / 3.0) * window(curvature, 0, cells_along + 1)
        )
    )
    upwind_right = courant_faces * (
        window(left_edge, 1, cells_along + 1)
        + 0.5
        * backward
        * (
            window(slopes, 1, cells_along + 1)
            + (1.0 - 2.0 * backward / 3.0) * window(curvature, 1, cells_along + 1)
        )
    )
    fluxes = jnp.where(courant_faces >= 0.0, upwind_left, upwind_right)
    return window(padded, 3, cells_along) - (
        window(fluxes, 1, cells_along) - window(fluxes, 0, cells_along)
    )


def pack_rows(tracer, north_wind, lowest):
    row_count = tracer.shape[3]
    width_cells = tracer.shape[4]
    if lowest:
        layers = tracer[:, :, :, 0:3, :]
        wind_row = north_wind[:, :, 0:1, :]
    else:
        layers = tracer[:, :, :, row_count - 3 :, :]
        wind_row = north_wind[:, :, row_count - 1 :, :]
    return jnp.concatenate([layers.reshape(-1, width_cells), wind_row.reshape(-1, width_cells)], 0)


def unpack_rows(packed, tracer_shape):
    split_at = tracer_shape[0] * tracer_shape[1] * 18
    layers = packed[:split_at].reshape(tracer_shape[0], tracer_shape[1], 6, 3, packed.shape[1])
    wind_row = packed[split_at:].reshape(tracer_shape[1], 6, packed.shape[1])
    return (layers, wind_row)


def column_halos(tracer, east_wind, north_wind, position, band_count):
    row_count = tracer.shape[3]
    width_cells = tracer.shape[4]
    received = []
    for root_rank, lowest in ((band_count - 1, False), (0, True)):
        packed = pack_rows(tracer, north_wind, lowest)
        received.append(unpack_rows(broadcast(packed, "space", root_rank), tracer.shape))
    top_layers, top_wind = received[0]
    low_layers, low_wind = received[1]
    start_column = width_cells - (position + 1) * row_count
    padded_faces = []
    speed_faces = []
    for face_number in range(6):
        if face_number % 2 == 0:
            source = lax.dynamic_slice_in_dim(
                top_layers[:, :, (face_number - 2) % 6], start_column, row_count, axis=3
            )
            west_cells = jnp.swapaxes(jnp.flip(source, -1), -1, -2)
            west_speed = jnp.flip(
                lax.dynamic_slice_in_dim(
                    top_wind[:, (face_number - 2) % 6], start_column, row_count, axis=1
                ),
                -1,
            )
            east_cells = tracer[:, :, (face_number + 1) % 6, :, 0:3]
            east_speed = east_wind[:, (face_number + 1) % 6, :, 0]
        else:
            west_cells = tracer[:, :, (face_number - 1) % 6, :, width_cells - 3 :]
            west_speed = east_wind[:, (face_number - 1) % 6, :, width_cells - 1]
            source = lax.dynamic_slice_in_dim(
                low_layers[:, :, (face_number + 2) % 6], start_column, row_count, axis=3
            )
            east_cells = jnp.swapaxes(jnp.flip(source, -1), -1, -2)
            east_speed = jnp.flip(
                lax.dynamic_slice_in_dim(
                    low_wind[:, (face_number + 2) % 6], start_column, row_count, axis=1
                ),
                -1,
            )
        padded_faces.append(
            jnp.concatenate([west_cells, tracer[:, :, face_number], east_cells], -1)
        )
        speeds = jnp.concatenate(
            [west_speed[:, :, None], east_wind[:, face_number], east_speed[:, :, None]], -1
        )
        speed_faces.append(0.5 * (speeds[:, :, :-1] + speeds[:, :, 1:]))
    return (jnp.stack(padded_faces, 2), jnp.stack(speed_faces, 1))


def row_halos(tracer, east_wind, north_wind, position, band_count):
    scenarios = tracer.shape[0]
    levels = tracer.shape[1]
    row_count = tracer.shape[3]
    width_cells = tracer.shape[4]
    shifted = []
    for step_by, lowest in ((-1, True), (1, False)):
        packed = pack_rows(tracer, north_wind, lowest)
        shifted.append(unpack_rows(from_behind(packed, "space", step_by), tracer.shape))
    above_layers, above_wind = shifted[0]
    below_layers, below_wind = shifted[1]
    columns = jnp.concatenate([tracer[..., 0:3], tracer[..., width_cells - 3 :]], -1)
    columns = jnp.swapaxes(columns, -1, -2).reshape(-1, row_count)
    column_speed = jnp.stack([east_wind[..., 0], east_wind[..., width_cells - 1]], -2).reshape(
        -1, row_count
    )
    gathered = lax.all_gather(
        jnp.concatenate([columns, column_speed], 0), "space", axis=1, tiled=True
    )
    split_at = scenarios * levels * 36
    edge_layers = gathered[:split_at].reshape(scenarios, levels, 6, 6, -1)
    edge_speed = gathered[split_at:].reshape(levels, 6, 2, -1)
    at_top = position == band_count - 1
    at_bottom = position == 0
    padded_faces = []
    speed_faces = []
    for face_number in range(6):
        if face_number % 2 == 0:
            north_cells = jnp.where(
                at_top,
                jnp.flip(edge_layers[:, :, (face_number + 2) % 6, 0:3], -1),
                above_layers[:, :, face_number],
            )
            north_speed = jnp.where(
                at_top,
                jnp.flip(edge_speed[:, (face_number + 2) % 6, 0], -1),
                above_wind[:, face_number],
            )
            south_cells = jnp.where(
                at_bottom,
                below_layers[:, :, (face_number - 1) % 6],
                below_layers[:, :, face_number],
            )
            south_speed = jnp.where(
                at_bottom, below_wind[:, (face_number - 1) % 6], below_wind[:, face_number]
            )
        else:
            north_cells = jnp.where(
                at_top, above_layers[:, :, (face_number + 1) % 6], above_layers[:, :, face_number]
            )
            north_speed = jnp.where(
                at_top, above_wind[:, (face_number + 1) % 6], above_wind[:, face_number]
            )
            south_cells = jnp.where(
                at_bottom,
                jnp.flip(edge_layers[:, :, (face_number - 2) % 6, 3:6], -1),
                below_layers[:, :, face_number],
            )
            south_speed = jnp.where(
                at_bottom,
                jnp.flip(edge_speed[:, (face_number - 2) % 6, 1], -1),
                below_wind[:, face_number],
            )
        padded_faces.append(
            jnp.concatenate([south_cells, tracer[:, :, face_number], north_cells], -2)
        )
        speeds = jnp.concatenate(
            [south_speed[:, None, :], north_wind[:, face_number], north_speed[:, None, :]], -2
        )
        speed_faces.append(0.5 * (speeds[:, :-1, :] + speeds[:, 1:, :]))
    return (jnp.stack(padded_faces, 2), jnp.stack(speed_faces, 1))


def local(concentration, emissions, courant, tile_source, tile_target, intersection):
    band_count = lax.axis_size("space")
    position = lax.axis_index("space")
    tracer = concentration.at[:, 0].add(emissions)
    east_wind = courant[0]
    north_wind = courant[1]
    for step_number in range(2):
        padded, courant_faces = column_halos(tracer, east_wind, north_wind, position, band_count)
        tracer = parabola_sweep(padded, courant_faces, 4)
        padded, courant_faces = row_halos(tracer, east_wind, north_wind, position, band_count)
        tracer = parabola_sweep(padded, courant_faces, 3)
    scenarios = tracer.shape[0]
    levels = tracer.shape[1]
    batch_rows = scenarios * levels
    block_cells = intersection.shape[1]
    blocks = tracer.astype(jnp.bfloat16).reshape(batch_rows, -1, block_cells)
    chosen = jnp.take(blocks, tile_source, axis=1)
    partial_value = jnp.einsum(
        "btk,tkc->tbc", chosen, intersection, preferred_element_type=jnp.float32
    )
    inside = (tile_target >= 0) & (tile_target < TGT_DEV * lax.axis_size("space"))
    slot_index = jnp.where(inside, tile_target, TGT_DEV * lax.axis_size("space"))
    empty = jnp.zeros((TGT_DEV * lax.axis_size("space"), batch_rows, block_cells), jnp.float32)
    summed = lax.psum_scatter(
        empty.at[slot_index].add(partial_value, mode="drop"),
        "space",
        scatter_dimension=0,
        tiled=True,
    )
    band_result = jnp.swapaxes(summed, 0, 1)
    regridded = band_result.reshape(scenarios, levels, TGT_DEV, block_cells)
    moment_sums = jnp.stack([jnp.sum(regridded, 0), jnp.sum(regridded * regridded, 0)])
    summed_moments = lax.psum(moment_sums, "scen")
    ensemble_moments = summed_moments / (scenarios * lax.axis_size("scen"))
    return (tracer, regridded, ensemble_moments)


def solution(mesh):
    return jax.shard_map(
        local,
        mesh=mesh,
        in_specs=(
            P("scen", None, None, "space", None),
            P("scen", None, "space", None),
            P(None, None, None, "space", None),
            P("space"),
            P("space"),
            P("space", None, None),
        ),
        out_specs=(
            P("scen", None, None, "space", None),
            P("scen", None, "space", None),
            P(None, None, "space", None),
        ),
        check_vma=False,
    )
```

profile of v0, /device:TPU:2, one launch (start us, length us, event | category | flops | bytes accessed | tf_op | source)
XLA Modules:
  0.0 1000.3 jit_solution(16481117192037455923)
XLA Ops:
  8.4 1.6 slice_bitcast_fusion
  12.5 1.7 fusion.60
  15.7 5.9 copy.2796
  21.6 7.1 fusion.179
  31.4 1.9 copy.2633
  34.1 2.6 copy.2637
  36.7 1.4 copy.2636
  38.1 2.6 copy.2641
  41.5 2.6 copy.2645
  44.8 2.6 copy.2649
  53.0 240.5 %all-reduce.10.cloned.1.call-done = (f32[192,384]{1,0:T(8,128)}, f32[192,384]{1,0:T(8,128)}) async-done(((f32[192,384]{1,0:T(8,128)}, f32[192,384]{1,0:T(8,128)}), (f32[192,384]{1,0:T(8,128)}, f32[192,384]{1,0:T(8,128)})) %all-reduce.10.cloned.1.call-update) | async-done | bytes 589840 | tf_op jit(solution)/shard_map/psum | solution.py:11
  296.3 1.5 slice.1216
  304.3 1.7 slice_subtract_fusion.1
  306.0 1.5 reshape.5219
  307.6 1.7 fusion.199
  316.5 1.9 bitcast_dynamic-update-slice_fusion.10
  318.4 1.8 constant_dynamic-update-slice_fusion.4
  320.2 1.8 bitcast_dynamic-update-slice_fusion.9
  327.7 2.7 fusion.17
  333.5 45.6 %all-gather = f32[32,12,384]{2,1,0:T(8,128)S(1)} all-gather(f32[1,12,384]{2,1,0:T(8,128)S(1)} %fusion.150), channel_id=1, replica_groups=mesh['space'=32,'scen'=8] {'space'}, dimensions={0}, use_global_device_ids=true | all-gather | bytes 608256 | tf_op jit(solution)/shard_map/all_gather | solution.py:143
  380.7 2.7 collective-permute-start.1
  407.0 275.7 %all-reduce.8.cloned.1.call-done = (f32[192,384]{1,0:T(8,128)}, f32[192,384]{1,0:T(8,128)}) async-done(((f32[192,384]{1,0:T(8,128)}, f32[192,384]{1,0:T(8,128)}), (f32[192,384]{1,0:T(8,128)}, f32[192,384]{1,0:T(8,128)})) %all-reduce.8.cloned.1.call-update) | async-done | bytes 589840 | tf_op jit(solution)/shard_map/psum | solution.py:11
  706.2 45.6 %all-gather.1 = f32[32,12,384]{2,1,0:T(8,128)S(1)} all-gather(f32[1,12,384]{2,1,0:T(8,128)S(1)} %fusion.151), channel_id=1, replica_groups=mesh['space'=32,'scen'=8] {'space'}, dimensions={0}, use_global_device_ids=true | all-gather | bytes 608256 | tf_op jit(solution)/shard_map/all_gather | solution.py:143
  753.1 2.6 collective-permute-start.3
  775.8 1.8 gather_fusion
  777.6 4.9 fusion.56
  782.5 2.3 broadcast_in_dim.40
  784.8 27.0 %scatter_fusion = f32[1024,8,128]{2,1,0:T(8,128)} fusion(f32[1024,8,128]{2,1,0:T(8,128)} %broadcast_in_dim.40, s32[270]{0:T(512)S(1)} %copy-done.76, f32[270,8,128]{2,1,0:T(8,128)S(1)} %fusion.56), kind=kCustom, calls=%fused_computation.1 | custom fusion | flops 276480 | bytes 3318840 | tf_op jit(solution)/shard_map/scatter-add | solution.py:224
  811.9 99.2 %reduce-scatter.2.cloned.1.call-done = f32[32,8,128]{2,1,0:T(8,128)} async-done(((f32[1024,8,128]{2,1,0:T(8,128)}), f32[32,8,128]{2,1,0:T(8,128)}) %reduce-scatter.2.cloned.1.call-update) | async-done | bytes 131088 | tf_op jit(solution)/shard_map/reduce_scatter | solution.py:223
  912.1 1.6 pad_maximum_fusion.8
  913.7 1.6 copy.2791
  915.3 76.8 %all-reduce.6.cloned.1.call-done = f32[2,8,32,128]{3,1,2,0:T(8,128)} async-done(((f32[2,8,32,128]{3,1,2,0:T(8,128)}), f32[2,8,32,128]{3,1,2,0:T(8,128)}) %all-reduce.6.cloned.1.call-update) | async-done | bytes 262160 | tf_op jit(solution)/shard_map/psum | solution.py:232
  (550 shorter events, 112.2 us)
Async XLA Ops:
  7.2 286.3 %all-reduce.10.cloned.1.call-start = ((), (), s32[]{:S(2)}) async-start(), calls=%async_computation.4 | async-start | bytes 1179648 | tf_op jit(solution)/shard_map/psum | solution.py:11
  14.9 667.8 %all-reduce.8.cloned.1.call-start = ((), (), s32[]{:S(2)}) async-start(), calls=%async_computation.3 | async-start | bytes 1179648 | tf_op jit(solution)/shard_map/psum | solution.py:11
  33.3 266.2 %copy-start.10 = (f32[8,1,12,384]{3,0,2,1:T(8,128)}, f32[8,1,12,384]{3,0,2,1:T(8,128)S(1)}, u32[]{:S(2)}) copy-start(f32[8,1,12,384]{3,0,2,1:T(8,128)S(1)} %copy.2633) | copy-start | bytes 442372
  34.1 265.4 %copy-start.35 = (f32[8,1,12,1]{3,0,2,1:T(8,128)}, f32[8,1,12,1]{3,0,2,1:T(8,128)S(1)}, u32[]{:S(2)}) copy-start(f32[8,1,12,1]{3,0,2,1:T(8,128)S(1)} %copy.2635) | copy-start | bytes 1156
  51.9 281.4 %copy-start.69 = (f32[96,12]{0,1:T(8,128)}, f32[96,12]{0,1:T(8,128)S(1)}, u32[]{:S(2)}) copy-start(f32[96,12]{0,1:T(8,128)S(1)} %copy.2662) | copy-start | bytes 13828
  316.5 5.5 copy-start.7
  316.5 5.5 copy-start.32
  316.5 5.5 copy-start.40
  316.5 6.4 copy-start.5
  316.5 6.4 copy-start.30
  316.5 6.4 copy-start.41
  318.4 6.1 copy-start.3
  318.4 6.1 copy-start.28
  318.4 6.1 copy-start.42
  322.0 4.0 copy-start.1
  322.0 4.0 copy-start.26
  322.0 4.0 copy-start.43
  332.7 59.0 %collective-permute-start = (f32[192,384]{1,0:T(8,128)}, f32[192,384]{1,0:T(8,128)}, u32[]{:S(2)}, u32[]{:S(2)}) collective-permute-start(f32[192,384]{1,0:T(8,128)} %pad_maximum_fusion.2), channel_id=1, source_target_pairs={{248,0},{0,8},{8,16},{16,24},{24,32},{32,40},{40,48},{48,56},{56,6... | collective-permute-start | bytes 884744 | tf_op jit(solution)/shard_map/ppermute | solution.py:17
  380.7 12.1 %collective-permute-start.1 = (f32[192,384]{1,0:T(8,128)}, f32[192,384]{1,0:T(8,128)S(1)}, u32[]{:S(2)}, u32[]{:S(2)}) collective-permute-start(f32[192,384]{1,0:T(8,128)} %pad_maximum_fusion.6), channel_id=1, source_target_pairs={{8,0},{16,8},{24,16},{32,24},{40,32},{48,40},{56,48},{64,56},{72,6... | collective-permute-start | bytes 884744 | tf_op jit(solution)/shard_map/ppermute | solution.py:17
  383.9 9.5 copy-start.17
  406.1 505.1 %reduce-scatter.2.cloned.1.call-start = ((), (), s32[]{:S(2)}) async-start(), calls=%async_computation.1 | async-start | bytes 4325376 | tf_op jit(solution)/shard_map/reduce_scatter | solution.py:223
  406.9 277.1 %copy-start.11 = (f32[8,1,12,384]{3,0,2,1:T(8,128)S(1)}, f32[8,1,12,384]{3,0,2,1:T(8,128)}, u32[]{:S(2)}) copy-start(f32[8,1,12,384]{3,0,2,1:T(8,128)} %copy-done.10) | copy-start | bytes 442372
  406.9 277.1 %copy-start.36 = (f32[8,1,12,1]{3,0,2,1:T(8,128)S(1)}, f32[8,1,12,1]{3,0,2,1:T(8,128)}, u32[]{:S(2)}) copy-start(f32[8,1,12,1]{3,0,2,1:T(8,128)} %copy-done.35) | copy-start | bytes 1156
  684.0 4.2 copy-start.9
  684.0 4.2 copy-start.34
  685.6 4.2 copy-start.8
  685.6 4.2 copy-start.33
  686.7 4.8 copy-start.6
  686.7 4.8 copy-start.31
  705.4 61.8 %collective-permute-start.2 = (f32[192,384]{1,0:T(8,128)}, f32[192,384]{1,0:T(8,128)}, u32[]{:S(2)}, u32[]{:S(2)}) collective-permute-start(f32[192,384]{1,0:T(8,128)} %pad_maximum_fusion), channel_id=1, source_target_pairs={{248,0},{0,8},{8,16},{16,24},{24,32},{32,40},{40,48},{48,56},{56,6... | collective-permute-start | bytes 884744 | tf_op jit(solution)/shard_map/ppermute | solution.py:17
  753.1 15.6 %collective-permute-start.3 = (f32[192,384]{1,0:T(8,128)}, f32[192,384]{1,0:T(8,128)S(1)}, u32[]{:S(2)}, u32[]{:S(2)}) collective-permute-start(f32[192,384]{1,0:T(8,128)} %pad_maximum_fusion.4), channel_id=1, source_target_pairs={{8,0},{16,8},{24,16},{32,24},{40,32},{48,40},{56,48},{64,56},{72,6... | collective-permute-start | bytes 884744 | tf_op jit(solution)/shard_map/ppermute | solution.py:17
  811.9 180.2 %all-reduce.6.cloned.1.call-start = ((), (), s32[]{:S(2)}) async-start(), calls=%async_computation.2 | async-start | bytes 524288 | tf_op jit(solution)/shard_map/psum | solution.py:232
  (55 other events, 100.5 us)
Sparse Core Ops, SparseCore 0:
  15.0 278.3 all-reduce.9
  406.2 276.4 all-reduce.7
  812.0 99.1 reduce-scatter.1
  914.2 77.8 all-reduce.5
where the time goes:
time: 1000 us
  waiting for transfers between devices  692 us (69%)
  local copies, waits for them, and re-layouts  112 us (11%)
  blocking collectives  91.1 us (9%)
  other arithmetic  78.5 us (8%)
  between operations  15.8 us (2%)
    psum x2, waiting for transfers between devices, broadcast(): return lax.psum(kept, axis)  516 us
    reduce_scatter x1, waiting for transfers between devices, local(): lax.psum_scatter(empty.at[slot_index].add(partial_value, mode='drop'), 's...  99.2 us
    all_gather x2, blocking collectives, row_halos(): lax.all_gather(jnp.concatenate([columns, column_speed], 0), 'space', axis...  91.1 us
    psum x1, waiting for transfers between devices, local(): summed_moments = lax.psum(moment_sums, 'scen')  76.8 us
    scatter-add x1, other arithmetic, local(): empty.at[slot_index].add(partial_value, mode='drop')  27 us
    unnamed x62, other arithmetic  21.1 us
    slice x7, local copies, waits for them, and re-layouts, column_halos(): east_wind[:, face_number]  20.5 us
  transfers between devices with their start and end apart: 8, of which 4 were waited for; matrix products, arithmetic and copies ran while one was open for 7% of the time, Pallas kernels for 0%

commit v1 on v0

--- a/solution.py
+++ b/solution.py
@@ -229,7 +229,8 @@
     band_result = jnp.swapaxes(summed, 0, 1)
     regridded = band_result.reshape(scenarios, levels, TGT_DEV, block_cells)
     moment_sums = jnp.stack([jnp.sum(regridded, 0), jnp.sum(regridded * regridded, 0)])
-    summed_moments = lax.psum(moment_sums, "scen")
+    parts = lax.all_gather(moment_sums, "scen", axis=0, tiled=False)
+    summed_moments = parts.sum(axis=0)
     ensemble_moments = summed_moments / (scenarios * lax.axis_size("scen"))
     return (tracer, regridded, ensemble_moments)
 

time: 1000 us -> 979 us (0.979)
  waiting for transfers between devices: 692 us -> 668 us
    psum x1 -> x0, waiting for transfers between devices: 76.8 us -> none  [local(): summed_moments = lax.psum(moment_sums, 'scen')]
    all_gather x0 -> x1, waiting for transfers between devices: none -> 52.9 us  [local(): parts = lax.all_gather(moment_sums, 'scen', axis=0, tiled=False)]
where the time goes in v1:
time: 979 us; the launch traced here: 977 us
  waiting for transfers between devices  668 us (68%)
  local copies, waits for them, and re-layouts  112 us (11%)
  blocking collectives  91.1 us (9%)
  other arithmetic  79 us (8%)
  between operations  15.8 us (2%)
    psum x2, waiting for transfers between devices, broadcast(): return lax.psum(kept, axis)  516 us
    reduce_scatter x1, waiting for transfers between devices, local(): lax.psum_scatter(empty.at[slot_index].add(partial_value, mode='drop'), 's...  99.3 us
    all_gather x2, blocking collectives, row_halos(): lax.all_gather(jnp.concatenate([columns, column_speed], 0), 'space', axis...  91.1 us
    all_gather x1, waiting for transfers between devices, local(): parts = lax.all_gather(moment_sums, 'scen', axis=0, tiled=False)  52.9 us
    scatter-add x1, other arithmetic, local(): empty.at[slot_index].add(partial_value, mode='drop')  27 us
    unnamed x62, other arithmetic  21.1 us
    slice x7, local copies, waits for them, and re-layouts, column_halos(): east_wind[:, face_number]  20.4 us
  transfers between devices with their start and end apart: 8, of which 4 were waited for; matrix products, arithmetic and copies ran while one was open for 7% of the time, Pallas kernels for 0%

profile of v1, /device:TPU:2, one launch (start us, length us, event | category | flops | bytes accessed | tf_op | source)
XLA Modules:
  0.0 976.8 jit_solution(3458232824893531727)
XLA Ops:
  8.4 1.6 slice_bitcast_fusion
  12.5 1.7 fusion.60
  15.7 5.8 copy.2788
  21.5 7.0 fusion.179
  31.3 1.9 copy.2622
  34.0 2.6 copy.2626
  38.0 2.6 copy.2630
  41.3 2.6 copy.2634
  44.6 2.6 copy.2638
  52.9 240.6 %all-reduce.7.cloned.1.call-done = (f32[192,384]{1,0:T(8,128)}, f32[192,384]{1,0:T(8,128)}) async-done(((f32[192,384]{1,0:T(8,128)}, f32[192,384]{1,0:T(8,128)}), (f32[192,384]{1,0:T(8,128)}, f32[192,384]{1,0:T(8,128)})) %all-reduce.7.cloned.1.call-update) | async-done | bytes 589840 | tf_op jit(solution)/shard_map/psum | solution.py:11
  296.3 1.5 slice.1216
  304.3 1.7 slice_subtract_fusion.1
  306.0 1.5 reshape.5219
  307.6 1.7 fusion.199
  316.5 1.9 bitcast_dynamic-update-slice_fusion.10
  318.4 1.8 constant_dynamic-update-slice_fusion.4
  320.2 1.8 bitcast_dynamic-update-slice_fusion.9
  327.7 2.7 fusion.17
  333.5 45.6 %all-gather.1 = f32[32,12,384]{2,1,0:T(8,128)S(1)} all-gather(f32[1,12,384]{2,1,0:T(8,128)S(1)} %fusion.150), channel_id=1, replica_groups=mesh['space'=32,'scen'=8] {'space'}, dimensions={0}, use_global_device_ids=true | all-gather | bytes 608256 | tf_op jit(solution)/shard_map/all_gather | solution.py:143
  380.7 2.7 collective-permute-start.1
  390.4 1.4 rev.164
  407.0 275.6 %all-reduce.5.cloned.1.call-done = (f32[192,384]{1,0:T(8,128)}, f32[192,384]{1,0:T(8,128)}) async-done(((f32[192,384]{1,0:T(8,128)}, f32[192,384]{1,0:T(8,128)}), (f32[192,384]{1,0:T(8,128)}, f32[192,384]{1,0:T(8,128)})) %all-reduce.5.cloned.1.call-update) | async-done | bytes 589840 | tf_op jit(solution)/shard_map/psum | solution.py:11
  706.2 45.6 %all-gather.2 = f32[32,12,384]{2,1,0:T(8,128)S(1)} all-gather(f32[1,12,384]{2,1,0:T(8,128)S(1)} %fusion.151), channel_id=1, replica_groups=mesh['space'=32,'scen'=8] {'space'}, dimensions={0}, use_global_device_ids=true | all-gather | bytes 608256 | tf_op jit(solution)/shard_map/all_gather | solution.py:143
  753.2 2.6 collective-permute-start.3
  763.4 1.4 rev.187
  775.8 1.8 gather_fusion
  777.6 4.9 fusion.56
  782.5 2.3 broadcast_in_dim.40
  784.8 27.0 %scatter_fusion = f32[1024,8,128]{2,1,0:T(8,128)} fusion(f32[1024,8,128]{2,1,0:T(8,128)} %broadcast_in_dim.40, s32[270]{0:T(512)S(1)} %copy-done.77, f32[270,8,128]{2,1,0:T(8,128)S(1)} %fusion.56), kind=kCustom, calls=%fused_computation.1 | custom fusion | flops 276480 | bytes 3318840 | tf_op jit(solution)/shard_map/scatter-add | solution.py:224
  812.0 99.3 %reduce-scatter.2.cloned.1.call-done = f32[32,8,128]{2,1,0:T(8,128)} async-done(((f32[1024,8,128]{2,1,0:T(8,128)}), f32[32,8,128]{2,1,0:T(8,128)}) %reduce-scatter.2.cloned.1.call-update) | async-done | bytes 131088 | tf_op jit(solution)/shard_map/reduce_scatter | solution.py:223
  914.7 52.9 %all-gather.5.cloned.1.call-done = f32[16,8,32,128]{3,2,1,0:T(8,128)} async-done(((f32[2,8,32,128]{3,2,1,0:T(8,128)}), f32[16,8,32,128]{3,2,1,0:T(8,128)}) %all-gather.5.cloned.1.call-update) | async-done | bytes 2097168 | tf_op jit(solution)/shard_map/all_gather | solution.py:232
  967.5 1.8 reduce_sum.8
  (554 shorter events, 112.6 us)
Async XLA Ops:
  7.2 286.3 %all-reduce.7.cloned.1.call-start = ((), (), s32[]{:S(2)}) async-start(), calls=%async_computation.4 | async-start | bytes 1179648 | tf_op jit(solution)/shard_map/psum | solution.py:11
  14.9 667.8 %all-reduce.5.cloned.1.call-start = ((), (), s32[]{:S(2)}) async-start(), calls=%async_computation.3 | async-start | bytes 1179648 | tf_op jit(solution)/shard_map/psum | solution.py:11
  33.2 266.4 %copy-start.10 = (f32[8,1,12,384]{3,0,2,1:T(8,128)}, f32[8,1,12,384]{3,0,2,1:T(8,128)S(1)}, u32[]{:S(2)}) copy-start(f32[8,1,12,384]{3,0,2,1:T(8,128)S(1)} %copy.2622) | copy-start | bytes 442372
  34.0 265.5 %copy-start.35 = (f32[8,1,12,1]{3,0,2,1:T(8,128)}, f32[8,1,12,1]{3,0,2,1:T(8,128)S(1)}, u32[]{:S(2)}) copy-start(f32[8,1,12,1]{3,0,2,1:T(8,128)S(1)} %copy.2624) | copy-start | bytes 1156
  51.9 281.6 %copy-start.70 = (f32[96,12]{0,1:T(8,128)}, f32[96,12]{0,1:T(8,128)S(1)}, u32[]{:S(2)}) copy-start(f32[96,12]{0,1:T(8,128)S(1)} %copy.2651) | copy-start | bytes 13828
  316.5 5.6 copy-start.7
  316.5 5.6 copy-start.32
  316.5 5.6 copy-start.41
  316.5 6.4 copy-start.5
  316.5 6.4 copy-start.30
  316.5 6.4 copy-start.42
  318.4 6.2 copy-start.3
  318.4 6.2 copy-start.28
  318.4 6.2 copy-start.43
  322.0 4.1 copy-start.1
  322.0 4.1 copy-start.26
  322.1 4.1 copy-start.44
  332.8 59.0 %collective-permute-start = (f32[192,384]{1,0:T(8,128)}, f32[192,384]{1,0:T(8,128)}, u32[]{:S(2)}, u32[]{:S(2)}) collective-permute-start(f32[192,384]{1,0:T(8,128)} %pad_maximum_fusion.2), channel_id=1, source_target_pairs={{248,0},{0,8},{8,16},{16,24},{24,32},{32,40},{40,48},{48,56},{56,6... | collective-permute-start | bytes 884744 | tf_op jit(solution)/shard_map/ppermute | solution.py:17
  380.7 12.0 %collective-permute-start.1 = (f32[192,384]{1,0:T(8,128)}, f32[192,384]{1,0:T(8,128)S(1)}, u32[]{:S(2)}, u32[]{:S(2)}) collective-permute-start(f32[192,384]{1,0:T(8,128)} %pad_maximum_fusion.6), channel_id=1, source_target_pairs={{8,0},{16,8},{24,16},{32,24},{40,32},{48,40},{56,48},{64,56},{72,6... | collective-permute-start | bytes 884744 | tf_op jit(solution)/shard_map/ppermute | solution.py:17
  384.0 9.5 copy-start.17
  406.1 505.1 %reduce-scatter.2.cloned.1.call-start = ((), (), s32[]{:S(2)}) async-start(), calls=%async_computation.1 | async-start | bytes 4325376 | tf_op jit(solution)/shard_map/reduce_scatter | solution.py:223
  407.0 277.0 %copy-start.11 = (f32[8,1,12,384]{3,0,2,1:T(8,128)S(1)}, f32[8,1,12,384]{3,0,2,1:T(8,128)}, u32[]{:S(2)}) copy-start(f32[8,1,12,384]{3,0,2,1:T(8,128)} %copy-done.10) | copy-start | bytes 442372
  407.0 277.0 %copy-start.36 = (f32[8,1,12,1]{3,0,2,1:T(8,128)S(1)}, f32[8,1,12,1]{3,0,2,1:T(8,128)}, u32[]{:S(2)}) copy-start(f32[8,1,12,1]{3,0,2,1:T(8,128)} %copy-done.35) | copy-start | bytes 1156
  684.0 4.2 copy-start.9
  684.0 4.2 copy-start.34
  685.6 4.2 copy-start.8
  685.6 4.2 copy-start.33
  686.6 4.8 copy-start.6
  686.6 4.8 copy-start.31
  705.5 61.8 %collective-permute-start.2 = (f32[192,384]{1,0:T(8,128)}, f32[192,384]{1,0:T(8,128)}, u32[]{:S(2)}, u32[]{:S(2)}) collective-permute-start(f32[192,384]{1,0:T(8,128)} %pad_maximum_fusion), channel_id=1, source_target_pairs={{248,0},{0,8},{8,16},{16,24},{24,32},{32,40},{40,48},{48,56},{56,6... | collective-permute-start | bytes 884744 | tf_op jit(solution)/shard_map/ppermute | solution.py:17
  753.2 15.6 %collective-permute-start.3 = (f32[192,384]{1,0:T(8,128)}, f32[192,384]{1,0:T(8,128)S(1)}, u32[]{:S(2)}, u32[]{:S(2)}) collective-permute-start(f32[192,384]{1,0:T(8,128)} %pad_maximum_fusion.4), channel_id=1, source_target_pairs={{8,0},{16,8},{24,16},{32,24},{40,32},{48,40},{56,48},{64,56},{72,6... | collective-permute-start | bytes 884744 | tf_op jit(solution)/shard_map/ppermute | solution.py:17
  811.9 155.6 %all-gather.5.cloned.1.call-start = ((), (), s32[]{:S(2)}) async-start(), calls=%async_computation.2 | async-start | bytes 2359296 | tf_op jit(solution)/shard_map/all_gather | solution.py:232
  (56 other events, 103.4 us)
Sparse Core Ops, SparseCore 0:
  15.0 278.4 all-reduce.6
  406.3 276.3 all-reduce.4
  812.0 99.1 reduce-scatter.1
  914.1 53.3 all-gather.4
